TPU v7x, 512 devices: a whole 4x4x16 slice. The times are simulated.
512 devices in a mesh: seq: 128 (over x, z, core), head: 4 (over y).
Axes of the slice: x: 4, y: 4, z: 16, core: 2. Of those that a mesh axis runs over, the one named last changes fastest.
Arguments:
- hidden: bfloat16 [32768, 2560], P(('seq', 'head')), may hold values from -6 to 6
- w_values: bfloat16 [2560, 2560], P('seq', 'head'), may hold values from -0.125 to 0.125
- w_gates: bfloat16 [2560, 2560], P('seq', 'head'), may hold values from -0.125 to 0.125
- w_steps: bfloat16 [2560, 40], P('seq', 'head'), may hold values from -0.0625 to 0.0625
- w_states: bfloat16 [2560, 256], P('seq'), may hold values from -0.125 to 0.125
- conv_weight: float32 [4, 2816], replicated, may hold values from -3 to 3
- conv_bias: float32 [2816], replicated, may hold values from -3 to 3
- step_bias: float32 [40], P('head'), may hold values from -1 to 0.5
- decay_rate: float32 [40], P('head'), may hold values from 0 to 1, as said below
- skip_gain: float32 [40], P('head'), may hold values from 1 to 8
- norm_gain: float32 [2560], replicated, may hold values from 0.5 to 1.5
- lengths: int32 [64], replicated, may hold values from 256 to 768, as said below
Outputs:
- gated_out: bfloat16 [32768, 2560], P(('seq', 'head'))
- final_states: float32 [128, 40, 64, 128], P('seq', 'head')
Inputs may be any that keep to these rules, and one draw needn't show every extreme that they name: Prompts are packed in order, each holding 256 to 768 tokens; the lengths sum to 32768. `decay_rate`: positive rates.
All inputs are finite; a program needn't handle non-finite values.
Results may differ from a plain program's by a relative error of at most 0.01.
Values may be sent and summed in bfloat16 or wider, within the bound.
No kernel may reach another device: no remote copies, remote signals or barrier semaphores. Data moves between devices by JAX's collectives and lax.ppermute only.
A program may use at most 128 MiB of HBM per device.

v0:
```python
import jax
import jax.numpy as jnp
from jax import lax
from jax.sharding import PartitionSpec as P

STRETCH = 256
epsilon = 1e-05


def from_behind(block, axis, distance):
    devices = range(lax.axis_size(axis))
    route = [(i - distance, i) for i in devices if i - distance in devices]
    return lax.ppermute(block, axis, route)


def segments_at(positions, prompt_ends):
    counted = jnp.sum((prompt_ends[None, :] <= positions[:, None]).astype(jnp.int32), axis=1)
    return jnp.where(positions < 0, -1, counted)


def on_device(
    hidden,
    w_values,
    w_gates,
    w_steps,
    w_states,
    conv_weight,
    conv_bias,
    step_bias,
    decay_rate,
    skip_gain,
    norm_gain,
    lengths,
):
    groups = lax.axis_size("head")
    group_index = lax.axis_index("head")
    block_index = lax.axis_index("seq")
    local_width = w_values.shape[1]
    inner_width = local_width * groups
    local_heads = decay_rate.shape[0]
    head_width = local_width // local_heads
    state_width = w_states.shape[1] // 2
    conv_taps = conv_weight.shape[0]
    prompt_ends = jnp.cumsum(lengths)
    block_hidden = lax.all_to_all(
        jnp.broadcast_to(hidden[None], (groups,) + hidden.shape), "head", 0, 0, tiled=True
    ).reshape(groups * hidden.shape[0], hidden.shape[1])
    block_rows = block_hidden.shape[0]
    sub_rows = block_rows // groups
    step_width = w_steps.shape[1]
    merged = jnp.concatenate([w_values, w_states, w_gates, w_steps], axis=1)
    full = lax.all_gather(merged, "seq", axis=0, tiled=True)
    projected = jnp.dot(block_hidden, full, preferred_element_type=jnp.float32)
    conv_end = local_width + 2 * state_width
    pre_rows = projected[:, :conv_end].astype(jnp.bfloat16)
    gates_sum = projected[:, conv_end : conv_end + local_width]
    steps_sum = projected[:, conv_end + local_width : conv_end + local_width + step_width]
    local_taps = jnp.concatenate(
        [
            lax.dynamic_slice_in_dim(conv_weight, group_index * local_width, local_width, 1),
            conv_weight[:, inner_width:],
        ],
        axis=1,
    )
    local_bias = jnp.concatenate(
        [
            lax.dynamic_slice_in_dim(conv_bias, group_index * local_width, local_width, 0),
            conv_bias[inner_width:],
        ],
        axis=0,
    )
    block_start = block_index * block_rows
    rim_rows = pre_rows[block_rows - (conv_taps - 1) :]
    prior_rim = from_behind(rim_rows, "seq", 1)
    extended = jnp.concatenate([prior_rim, pre_rows], axis=0)
    ext_positions = (
        block_start - (conv_taps - 1) + jnp.arange(block_rows + conv_taps - 1, dtype=jnp.int32)
    )
    ext_ids = segments_at(ext_positions, prompt_ends)
    own_ids = ext_ids[conv_taps - 1 :]
    filtered = jnp.zeros(pre_rows.shape, jnp.float32) + local_bias[None, :]
    for offset in range(conv_taps):
        matches = (ext_ids[offset : offset + block_rows] == own_ids).astype(jnp.float32)
        filtered = (
            filtered
            + local_taps[offset][None, :]
            * extended[offset : offset + block_rows].astype(jnp.float32)
            * matches[:, None]
        )
    conv_out = jax.nn.silu(filtered).astype(jnp.bfloat16)
    head_values = conv_out[:, :local_width]
    both_states = conv_out[:, local_width:]
    stretch_rows = STRETCH
    stretches = block_rows // stretch_rows
    positions = block_start + jnp.arange(block_rows, dtype=jnp.int32)
    segment_ids = segments_at(positions, prompt_ends)
    next_ids = segments_at(positions + 1, prompt_ends)
    before_ids = segments_at(positions - 1, prompt_ends)
    stretch_ids = segment_ids.reshape(stretches, stretch_rows)
    prior_ids = before_ids.reshape(stretches, stretch_rows)[:, 0]
    ends_mask = (segment_ids != next_ids).reshape(stretches, stretch_rows)
    step_sizes = jax.nn.softplus(steps_sum + step_bias[None, :])
    decay_steps = step_sizes * decay_rate[None, :]
    log_decay = -jnp.cumsum(decay_steps.reshape(stretches, stretch_rows, local_heads), axis=1)
    decay_heads = jnp.swapaxes(log_decay, 1, 2)
    step_heads = jnp.swapaxes(step_sizes.reshape(stretches, stretch_rows, local_heads), 1, 2)
    values = head_values.reshape(stretches, stretch_rows, local_heads, head_width)
    write_state = both_states[:, :state_width].reshape(stretches, stretch_rows, state_width)
    read_state = both_states[:, state_width:].reshape(stretches, stretch_rows, state_width)
    intersection = jnp.einsum(
        "ctn,csn->cts", read_state, write_state, preferred_element_type=jnp.float32
    )
    token_order = jnp.arange(stretch_rows, dtype=jnp.int32)
    causal = token_order[:, None] >= token_order[None, :]
    allowed = causal[None] & (stretch_ids[:, :, None] == stretch_ids[:, None, :])
    spread = decay_heads[:, :, :, None] - decay_heads[:, :, None, :]
    weights = (
        jnp.where(allowed[:, None], jnp.exp(jnp.minimum(spread, 0.0)), 0.0)
        * step_heads[:, :, None, :]
    )
    scores = (intersection[:, None] * weights).astype(jnp.bfloat16)
    within_stretch = jnp.einsum(
        "chts,cshp->cthp", scores, values, preferred_element_type=jnp.float32
    )
    last_ids = stretch_ids[:, -1]
    tail_decay = decay_heads[:, :, -1:]
    keep_tail = (stretch_ids == last_ids[:, None])[:, None, :]
    tail_coef = (
        jnp.where(keep_tail, jnp.exp(jnp.minimum(tail_decay - decay_heads, 0.0)), 0.0) * step_heads
    )
    tail_rows = (values.astype(jnp.float32) * jnp.swapaxes(tail_coef, 1, 2)[:, :, :, None]).astype(
        jnp.bfloat16
    )
    stretch_states = jnp.einsum(
        "clhp,cln->chpn", tail_rows, write_state, preferred_element_type=jnp.float32
    )
    stretch_gates = (
        jnp.exp(decay_heads[:, :, -1]) * (last_ids == prior_ids).astype(jnp.float32)[:, None]
    )
    own_pair = (stretch_gates[0], stretch_states[0])
    g1, s1 = from_behind(own_pair, "seq", 1)
    g2, s2 = from_behind(own_pair, "seq", 2)
    g3, s3 = from_behind(own_pair, "seq", 3)
    incoming = s1 + g1[:, None, None] * (s2 + g2[:, None, None] * s3)
    arriving = incoming[None]
    carry_mask = (stretch_ids == prior_ids[:, None]).astype(jnp.float32)
    carry_decay = jnp.exp(log_decay) * carry_mask[:, :, None]
    from_before = (
        jnp.einsum(
            "cln,chpn->clhp",
            read_state,
            arriving.astype(jnp.bfloat16),
            preferred_element_type=jnp.float32,
        )
        * carry_decay[:, :, :, None]
    )
    result = (
        within_stretch + from_before + skip_gain[None, None, :, None] * values.astype(jnp.float32)
    )
    ssm_rows = result.reshape(block_rows, local_width).astype(jnp.bfloat16)
    end_weight = ends_mask.astype(jnp.float32)
    has_end = jnp.sum(end_weight, axis=1)
    end_decay = jnp.sum(decay_heads * end_weight[:, None, :], axis=2)
    end_ids = jnp.sum(jnp.where(ends_mask, stretch_ids, 0), axis=1)
    keep_end = ((stretch_ids == end_ids[:, None]) & (has_end[:, None] > 0))[:, None, :]
    end_coef = (
        jnp.where(keep_end, jnp.exp(jnp.minimum(end_decay[:, :, None] - decay_heads, 0.0)), 0.0)
        * step_heads
    )
    end_rows = (values.astype(jnp.float32) * jnp.swapaxes(end_coef, 1, 2)[:, :, :, None]).astype(
        jnp.bfloat16
    )
    end_states = jnp.einsum(
        "clhp,cln->chpn", end_rows, write_state, preferred_element_type=jnp.float32
    )
    end_carry = (
        jnp.exp(end_decay) * ((end_ids == prior_ids) & (has_end > 0)).astype(jnp.float32)[:, None]
    )
    end_states = end_states + end_carry[:, :, None, None] * arriving
    final_block = jnp.sum(end_states, axis=0)[None]
    head_gates = gates_sum.astype(jnp.bfloat16)
    both = jnp.stack([ssm_rows, head_gates]).reshape(2, groups, sub_rows, local_width)
    returned = lax.all_to_all(both, "head", split_axis=1, concat_axis=3, tiled=True)
    token_rows = returned.reshape(2, sub_rows, inner_width).astype(jnp.float32)
    gated = token_rows[0] * jax.nn.silu(token_rows[1])
    mean_square = jnp.mean(gated * gated, axis=1)
    scaled = gated * lax.rsqrt(mean_square + epsilon)[:, None] * norm_gain[None, :]
    gated_out = scaled.astype(jnp.bfloat16)
    return (gated_out, final_block)


def solution(mesh):
    in_specs = (
        P(("seq", "head"), None),
        P("seq", "head"),
        P("seq", "head"),
        P("seq", "head"),
        P("seq", None),
        P(),
        P(),
        P("head"),
        P("head"),
        P("head"),
        P(),
        P(),
    )
    out_specs = (P(("seq", "head"), None), P("seq", "head", None, None))
    return jax.shard_map(
        on_device, mesh=mesh, in_specs=in_specs, out_specs=out_specs, check_vma=False
    )
```

profile of v0, /device:TPU:5, one launch (start us, length us, event | category | flops | bytes accessed | tf_op | source)
XLA Modules:
  0.0 259.8 jit_solution(16076834221550302030)
XLA Ops:
  7.2 0.8 copy.65
  8.0 1.4 maximum_bitcast_fusion
  9.5 2.1 broadcast_in_dim.39
  11.6 4.3 %all-to-all-start = ((bf16[4,64,2560]{2,1,0:T(8,128)(2,1)}), bf16[4,64,2560]{2,1,0:T(8,128)(2,1)S(1)}, u32[]{:S(2)}, u32[]{:S(2)}) async-start(bf16[4,64,2560]{2,1,0:T(8,128)(2,1)} %broadcast_in_dim.39), calls=%async_computation | async-start | bytes 2621440 | tf_op jit(solution)/shard_map/all_to_all | solution.py:45
  16.2 0.7 slice.91
  16.9 0.8 dynamic_slice.6
  24.3 0.7 broadcast_compare_fusion
  25.1 139.3 %all-gather.3.cloned.1.call-done = bf16[128,20,1546]{2,1,0:T(8,128)(2,1)} async-done(((bf16[1,20,1546]{2,1,0:T(8,128)(2,1)}), bf16[128,20,1546]{2,1,0:T(8,128)(2,1)}) %all-gather.3.cloned.1.call-update) | async-done | bytes 7915536 | tf_op jit(solution)/shard_map/all_gather | solution.py:52
  164.5 13.7 %reshape.504 = bf16[2560,1546]{1,0:T(8,128)(2,1)} reshape(bf16[128,20,1546]{2,1,0:T(8,128)(2,1)} %all-gather.3.cloned.1.call-done) | data formatting | bytes 15831040
  178.2 5.8 %fusion.50 = (bf16[256,1546]{0,1:T(8,128)(2,1)S(1)}, f32[256,1546]{0,1:T(8,128)S(1)}) fusion(bf16[2560,1546]{1,0:T(8,128)(2,1)} %reshape.504, bf16[256,2560]{1,0:T(8,128)(2,1)S(1)} %bitcast.126), kind=kOutput, calls=%fused_computation.113 | convolution fusion | flops 2026768896 | bytes 11600896 | tf_op jit(solution)/shard_map/dot_general | solution.py:53
  184.2 1.0 copy-done.4
  186.4 0.8 fusion.31
  187.4 3.4 %collective-permute-start.4 = (f32[10]{0:T(128)S(1)}, f32[10]{0:T(128)S(1)}, u32[]{:S(2)}, u32[]{:S(2)}) collective-permute-start(f32[10]{0:T(128)S(1)} %exponential_multiply_fusion.1), channel_id=1, source_target_pairs={{0,8},{4,12},{8,16},{12,20},{16,24},{20,28},{24,32},{28,36},{32,40... | collective-permute-start | bytes 128 | tf_op jit(solution)/shard_map/ppermute | solution.py:13
  190.8 2.8 %collective-permute-start.2 = (f32[10]{0:T(128)S(1)}, f32[10]{0:T(128)S(1)}, u32[]{:S(2)}, u32[]{:S(2)}) collective-permute-start(f32[10]{0:T(128)S(1)} %exponential_multiply_fusion.1), channel_id=1, source_target_pairs={{0,4},{4,8},{8,12},{12,16},{16,20},{20,24},{24,28},{28,32},{32,36}... | collective-permute-start | bytes 128 | tf_op jit(solution)/shard_map/ppermute | solution.py:13
  193.8 1.9 collective-permute-start
  195.8 0.8 fusion.32
  196.9 0.8 copy.75
  197.7 0.9 collective-permute-done
  198.7 1.5 multiply_convert_fusion.4
  200.2 0.8 fusion.12
  201.3 4.4 %collective-permute-start.1 = (f32[10,64,128]{2,1,0:T(8,128)S(1)}, f32[10,64,128]{2,1,0:T(8,128)S(1)}, u32[]{:S(2)}, u32[]{:S(2)}) collective-permute-start(f32[10,64,128]{2,1,0:T(8,128)S(1)} %fusion.20), channel_id=1, source_target_pairs={{0,4},{4,8},{8,12},{12,16},{16,20},{20,24},{24,28},{28,32},{32,36}... | collective-permute-start | bytes 983048 | tf_op jit(solution)/shard_map/ppermute | solution.py:13
  205.7 3.0 %collective-permute-start.3 = (f32[10,64,128]{2,1,0:T(8,128)S(1)}, f32[10,64,128]{2,1,0:T(8,128)S(1)}, u32[]{:S(2)}, u32[]{:S(2)}) collective-permute-start(f32[10,64,128]{2,1,0:T(8,128)S(1)} %fusion.20), channel_id=1, source_target_pairs={{0,8},{4,12},{8,16},{12,20},{16,24},{20,28},{24,32},{28,36},{32,40... | collective-permute-start | bytes 983048 | tf_op jit(solution)/shard_map/ppermute | solution.py:13
  208.7 2.5 collective-permute-start.5
  211.4 0.9 fusion.7
  212.4 11.8 %collective-permute-done.3 = f32[10,64,128]{2,1,0:T(8,128)S(1)} collective-permute-done((f32[10,64,128]{2,1,0:T(8,128)S(1)}, f32[10,64,128]{2,1,0:T(8,128)S(1)}, u32[]{:S(2)}, u32[]{:S(2)}) %collective-permute-start.3) | collective-permute-done | bytes 327712 | tf_op jit(solution)/shard_map/ppermute | solution.py:13
  224.2 7.7 %collective-permute-done.5 = f32[10,64,128]{2,1,0:T(8,128)S(1)} collective-permute-done((f32[10,64,128]{2,1,0:T(8,128)S(1)}, f32[10,64,128]{2,1,0:T(8,128)S(1)}, u32[]{:S(2)}, u32[]{:S(2)}) %collective-permute-start.5) | collective-permute-done | bytes 327712 | tf_op jit(solution)/shard_map/ppermute | solution.py:13
  232.6 1.1 pad_maximum_fusion
  233.7 2.4 copy.76
  236.1 4.0 %all-to-all-start.1 = ((bf16[2,4,64,640]{3,2,0,1:T(8,128)(2,1)}), bf16[2,4,64,640]{3,2,0,1:T(8,128)(2,1)S(1)}, u32[]{:S(2)}, u32[]{:S(2)}) async-start(bf16[2,4,64,640]{3,2,0,1:T(8,128)(2,1)} %copy.76), calls=%async_computation.1 | async-start | bytes 1310720 | tf_op jit(solution)/shard_map/all_to_all | solution.py:183
  240.8 1.0 add_bitcast_fusion
  241.8 8.4 %all-to-all-done.1 = bf16[2,4,64,640]{3,2,0,1:T(8,128)(2,1)S(1)} async-done(((bf16[2,4,64,640]{3,2,0,1:T(8,128)(2,1)}), bf16[2,4,64,640]{3,2,0,1:T(8,128)(2,1)S(1)}, u32[]{:S(2)}, u32[]{:S(2)}) %all-to-all-start.1) | async-done | bytes 655392 | tf_op jit(solution)/shard_map/all_to_all | solution.py:183
  252.1 0.8 multiply_convert_fusion.5
  (84 shorter events, 8.7 us)
Async XLA Ops:
  7.2 157.3 %all-gather.3.cloned.1.call-start = ((), (), s32[]{:S(2)}) async-start(), calls=%async_computation.2 | async-start | bytes 10303488 | tf_op jit(solution)/shard_map/all_gather | solution.py:52
  11.6 4.3 %copy-start.5 = (s32[64]{0:T(128)S(1)}, s32[64]{0:T(128)}, u32[]{:S(2)}) copy-start(s32[64]{0:T(128)} %param.23) | copy-start | bytes 772
  11.6 11.8 %copy-start.1 = (f32[4,2816]{1,0:T(4,128)S(1)}, f32[4,2816]{1,0:T(4,128)}, u32[]{:S(2)}) copy-start(f32[4,2816]{1,0:T(4,128)} %param.17) | copy-start | bytes 135172
  11.6 11.8 %slice-start = ((f32[4,2816]{1,0:T(4,128)}), f32[4,256]{1,0:T(4,128)S(1)}, s32[]{:S(2)}) async-start(f32[4,2816]{1,0:T(4,128)} %param.17), calls=%async_computation.3 | async-start | bytes 8192 | tf_op jit(solution)/shard_map/slice | solution.py:61
  11.6 166.6 %all-to-all-start = ((bf16[4,64,2560]{2,1,0:T(8,128)(2,1)}), bf16[4,64,2560]{2,1,0:T(8,128)(2,1)S(1)}, u32[]{:S(2)}, u32[]{:S(2)}) async-start(bf16[4,64,2560]{2,1,0:T(8,128)(2,1)} %broadcast_in_dim.39), calls=%async_computation | async-start | bytes 2621440 | tf_op jit(solution)/shard_map/all_to_all | solution.py:45
  178.2 5.9 %copy-start.3 = (f32[10]{0:T(128)S(1)}, f32[10]{0:T(128)}, u32[]{:S(2)}) copy-start(f32[10]{0:T(128)} %param.19) | copy-start | bytes 124
  178.2 5.9 %copy-start.6 = (f32[10]{0:T(128)S(1)}, f32[10]{0:T(128)}, u32[]{:S(2)}) copy-start(f32[10]{0:T(128)} %param.20) | copy-start | bytes 124
  184.0 1.2 copy-start.4
  187.4 24.9 %collective-permute-start.4 = (f32[10]{0:T(128)S(1)}, f32[10]{0:T(128)S(1)}, u32[]{:S(2)}, u32[]{:S(2)}) collective-permute-start(f32[10]{0:T(128)S(1)} %exponential_multiply_fusion.1), channel_id=1, source_target_pairs={{0,8},{4,12},{8,16},{12,20},{16,24},{20,28},{24,32},{28,36},{32,40... | collective-permute-start | bytes 128 | tf_op jit(solution)/shard_map/ppermute | solution.py:13
  190.8 21.5 %collective-permute-start.2 = (f32[10]{0:T(128)S(1)}, f32[10]{0:T(128)S(1)}, u32[]{:S(2)}, u32[]{:S(2)}) collective-permute-start(f32[10]{0:T(128)S(1)} %exponential_multiply_fusion.1), channel_id=1, source_target_pairs={{0,4},{4,8},{8,12},{12,16},{16,20},{20,24},{24,28},{28,32},{32,36}... | collective-permute-start | bytes 128 | tf_op jit(solution)/shard_map/ppermute | solution.py:13
  193.8 4.9 %collective-permute-start = (bf16[3,896]{0,1:T(8,128)(2,1)S(1)}, bf16[3,896]{0,1:T(8,128)(2,1)S(1)}, u32[]{:S(2)}, u32[]{:S(2)}) collective-permute-start(bf16[3,896]{0,1:T(8,128)(2,1)S(1)} %slice.120), channel_id=1, source_target_pairs={{0,4},{4,8},{8,12},{12,16},{16,20},{20,24},{24,28},{28,32},{32,36}... | collective-permute-start | bytes 16136 | tf_op jit(solution)/shard_map/ppermute | solution.py:13
  201.3 11.0 %collective-permute-start.1 = (f32[10,64,128]{2,1,0:T(8,128)S(1)}, f32[10,64,128]{2,1,0:T(8,128)S(1)}, u32[]{:S(2)}, u32[]{:S(2)}) collective-permute-start(f32[10,64,128]{2,1,0:T(8,128)S(1)} %fusion.20), channel_id=1, source_target_pairs={{0,4},{4,8},{8,12},{12,16},{16,20},{20,24},{24,28},{28,32},{32,36}... | collective-permute-start | bytes 983048 | tf_op jit(solution)/shard_map/ppermute | solution.py:13
  205.7 18.5 %collective-permute-start.3 = (f32[10,64,128]{2,1,0:T(8,128)S(1)}, f32[10,64,128]{2,1,0:T(8,128)S(1)}, u32[]{:S(2)}, u32[]{:S(2)}) collective-permute-start(f32[10,64,128]{2,1,0:T(8,128)S(1)} %fusion.20), channel_id=1, source_target_pairs={{0,8},{4,12},{8,16},{12,20},{16,24},{20,28},{24,32},{28,36},{32,40... | collective-permute-start | bytes 983048 | tf_op jit(solution)/shard_map/ppermute | solution.py:13
  208.7 23.2 %collective-permute-start.5 = (f32[10,64,128]{2,1,0:T(8,128)S(1)}, f32[10,64,128]{2,1,0:T(8,128)S(1)}, u32[]{:S(2)}, u32[]{:S(2)}) collective-permute-start(f32[10,64,128]{2,1,0:T(8,128)S(1)} %fusion.20), channel_id=1, source_target_pairs={{0,12},{4,16},{8,20},{12,24},{16,28},{20,32},{24,36},{28,40},{32,4... | collective-permute-start | bytes 983048 | tf_op jit(solution)/shard_map/ppermute | solution.py:13
  211.4 20.7 %copy-start.7 = (f32[10]{0:T(128)S(1)}, f32[10]{0:T(128)}, u32[]{:S(2)}) copy-start(f32[10]{0:T(128)} %param.21) | copy-start | bytes 124
  233.7 7.1 %copy-start = (bf16[256,640]{0,1:T(8,128)(2,1)S(1)}, bf16[256,640]{0,1:T(8,128)(2,1)}, u32[]{:S(2)}) copy-start(bf16[256,640]{0,1:T(8,128)(2,1)} %get-tuple-element.20) | copy-start | bytes 983044
  236.1 14.1 %all-to-all-start.1 = ((bf16[2,4,64,640]{3,2,0,1:T(8,128)(2,1)}), bf16[2,4,64,640]{3,2,0,1:T(8,128)(2,1)S(1)}, u32[]{:S(2)}, u32[]{:S(2)}) async-start(bf16[2,4,64,640]{3,2,0,1:T(8,128)(2,1)} %copy.76), calls=%async_computation.1 | async-start | bytes 1310720 | tf_op jit(solution)/shard_map/all_to_all | solution.py:183
  251.4 0.7 copy-start.2
Sparse Core Ops, SparseCore 0:
  11.7 152.7 all-gather.2
where the time goes:
time: 261 us; the launch traced here: 260 us
  waiting for transfers between devices  168 us (64%)
  local copies, waits for them, and re-layouts  26.9 us (10%)
  starting transfers between devices  26.3 us (10%)
  between operations  18.4 us (7%)
  other arithmetic  11.4 us (4%)
  matrix products  8.44 us (3%)
    all_gather x1, waiting for transfers between devices, on_device(): full = lax.all_gather(merged, 'seq', axis=0, tiled=True)  139 us
    ppermute x6, waiting for transfers between devices, from_behind(): return lax.ppermute(block, axis, route)  20.5 us
    ppermute x6, starting transfers between devices, from_behind(): return lax.ppermute(block, axis, route)  18 us
    unnamed x24, local copies, waits for them, and re-layouts  16 us
    all_to_all x1, waiting for transfers between devices, on_device(): lax.all_to_all(both, 'head', split_axis=1, concat_axis=3, tiled=True)  8.45 us
    dot_general x1, matrix products, on_device(): projected = jnp.dot(block_hidden, full, preferred_element_type=jnp.float32)  5.84 us
  transfers between devices with their start and end apart: 9, of which 5 were waited for; matrix products, arithmetic and copies ran while one was open for 11% of the time, Pallas kernels for 0%

commit v1 on v0

--- a/solution.py
+++ b/solution.py
@@ -180,7 +180,15 @@
     final_block = jnp.sum(end_states, axis=0)[None]
     head_gates = gates_sum.astype(jnp.bfloat16)
     both = jnp.stack([ssm_rows, head_gates]).reshape(2, groups, sub_rows, local_width)
-    returned = lax.all_to_all(both, "head", split_axis=1, concat_axis=3, tiled=True)
+    returned = jnp.concatenate(
+        lax.all_to_all(
+            jnp.stack(jnp.split(both, lax.psum(1, "head"), axis=1)),
+            "head",
+            split_axis=0,
+            concat_axis=0,
+        ),
+        axis=3,
+    )
     token_rows = returned.reshape(2, sub_rows, inner_width).astype(jnp.float32)
     gated = token_rows[0] * jax.nn.silu(token_rows[1])
     mean_square = jnp.mean(gated * gated, axis=1)

time: 261 us -> 268 us (1.027)
  other arithmetic: 11.4 us -> 17.7 us
    another operation x1, other arithmetic: 1.1 us -> 6.54 us  [on_device(): jnp.stack([ssm_rows, head_gates]).reshape(2, groups, sub_rows, local_width)]
    unnamed x24 -> x26, local copies, waits for them, and re-layouts: 16 us -> 16 us
where the time goes in v1:
time: 268 us; the launch traced here: 267 us
  waiting for transfers between devices  168 us (63%)
  local copies, waits for them, and re-layouts  27.9 us (10%)
  starting transfers between devices  26.3 us (10%)
  between operations  18.3 us (7%)
  other arithmetic  17.7 us (7%)
  matrix products  8.43 us (3%)
    all_gather x1, waiting for transfers between devices, on_device(): full = lax.all_gather(merged, 'seq', axis=0, tiled=True)  139 us
    ppermute x6, waiting for transfers between devices, from_behind(): return lax.ppermute(block, axis, route)  20.1 us
    ppermute x6, starting transfers between devices, from_behind(): return lax.ppermute(block, axis, route)  18 us
    unnamed x26, local copies, waits for them, and re-layouts  16 us
    all_to_all x1, waiting for transfers between devices, on_device(): lax.all_to_all(jnp.stack(jnp.split(both, lax.psum(1, 'head'), axis=1)), '...  8.55 us
    another operation x1, other arithmetic, on_device(): jnp.stack([ssm_rows, head_gates]).reshape(2, groups, sub_rows, local_width)  6.54 us
    dot_general x1, matrix products, on_device(): projected = jnp.dot(block_hidden, full, preferred_element_type=jnp.float32)  5.84 us
  transfers between devices with their start and end apart: 9, of which 5 were waited for; matrix products, arithmetic and copies ran while one was open for 11% of the time, Pallas kernels for 0%

profile of v1, /device:TPU:5, one launch (start us, length us, event | category | flops | bytes accessed | tf_op | source)
XLA Modules:
  0.0 266.8 jit_solution(9039778688504044191)
XLA Ops:
  7.2 0.8 copy.139
  8.0 1.4 maximum_bitcast_fusion
  9.5 2.1 broadcast_in_dim.39
  11.6 4.3 %all-to-all-start = ((bf16[4,64,2560]{2,1,0:T(8,128)(2,1)}), bf16[4,64,2560]{2,1,0:T(8,128)(2,1)S(1)}, u32[]{:S(2)}, u32[]{:S(2)}) async-start(bf16[4,64,2560]{2,1,0:T(8,128)(2,1)} %broadcast_in_dim.39), calls=%async_computation | async-start | bytes 2621440 | tf_op jit(solution)/shard_map/all_to_all | solution.py:45
  16.2 0.7 slice.91
  16.9 0.8 dynamic_slice.6
  25.0 139.4 %all-gather.3.cloned.1.call-done = bf16[128,20,1546]{2,1,0:T(8,128)(2,1)} async-done(((bf16[1,20,1546]{2,1,0:T(8,128)(2,1)}), bf16[128,20,1546]{2,1,0:T(8,128)(2,1)}) %all-gather.3.cloned.1.call-update) | async-done | bytes 7915536 | tf_op jit(solution)/shard_map/all_gather | solution.py:52
  164.5 13.7 %reshape.500 = bf16[2560,1546]{1,0:T(8,128)(2,1)} reshape(bf16[128,20,1546]{2,1,0:T(8,128)(2,1)} %all-gather.3.cloned.1.call-done) | data formatting | bytes 15831040
  178.2 5.8 %fusion.53 = (bf16[256,1546]{0,1:T(8,128)(2,1)S(1)}, f32[256,1546]{0,1:T(8,128)S(1)}) fusion(bf16[2560,1546]{1,0:T(8,128)(2,1)} %reshape.500, bf16[256,2560]{1,0:T(8,128)(2,1)S(1)} %bitcast.127), kind=kOutput, calls=%fused_computation.123 | convolution fusion | flops 2026768896 | bytes 11600896 | tf_op jit(solution)/shard_map/dot_general | solution.py:53
  184.2 1.0 copy-done.5
  186.4 0.8 fusion.34
  187.4 3.4 %collective-permute-start.4 = (f32[10]{0:T(128)S(1)}, f32[10]{0:T(128)S(1)}, u32[]{:S(2)}, u32[]{:S(2)}) collective-permute-start(f32[10]{0:T(128)S(1)} %exponential_multiply_fusion.1), channel_id=1, source_target_pairs={{0,8},{4,12},{8,16},{12,20},{16,24},{20,28},{24,32},{28,36},{32,40... | collective-permute-start | bytes 128 | tf_op jit(solution)/shard_map/ppermute | solution.py:13
  190.8 2.8 %collective-permute-start.2 = (f32[10]{0:T(128)S(1)}, f32[10]{0:T(128)S(1)}, u32[]{:S(2)}, u32[]{:S(2)}) collective-permute-start(f32[10]{0:T(128)S(1)} %exponential_multiply_fusion.1), channel_id=1, source_target_pairs={{0,4},{4,8},{8,12},{12,16},{16,20},{20,24},{24,28},{28,32},{32,36}... | collective-permute-start | bytes 128 | tf_op jit(solution)/shard_map/ppermute | solution.py:13
  193.8 1.9 collective-permute-start
  195.8 0.8 fusion.35
  196.9 1.3 copy.149
  198.7 1.5 multiply_convert_fusion.4
  200.2 0.8 fusion.15
  201.3 4.4 %collective-permute-start.1 = (f32[10,64,128]{2,1,0:T(8,128)S(1)}, f32[10,64,128]{2,1,0:T(8,128)S(1)}, u32[]{:S(2)}, u32[]{:S(2)}) collective-permute-start(f32[10,64,128]{2,1,0:T(8,128)S(1)} %fusion.23), channel_id=1, source_target_pairs={{0,4},{4,8},{8,12},{12,16},{16,20},{20,24},{24,28},{28,32},{32,36}... | collective-permute-start | bytes 983048 | tf_op jit(solution)/shard_map/ppermute | solution.py:13
  205.7 3.0 %collective-permute-start.3 = (f32[10,64,128]{2,1,0:T(8,128)S(1)}, f32[10,64,128]{2,1,0:T(8,128)S(1)}, u32[]{:S(2)}, u32[]{:S(2)}) collective-permute-start(f32[10,64,128]{2,1,0:T(8,128)S(1)} %fusion.23), channel_id=1, source_target_pairs={{0,8},{4,12},{8,16},{12,20},{16,24},{20,28},{24,32},{28,36},{32,40... | collective-permute-start | bytes 983048 | tf_op jit(solution)/shard_map/ppermute | solution.py:13
  208.7 2.5 collective-permute-start.5
  211.4 0.9 fusion.7
  212.4 11.8 %collective-permute-done.3 = f32[10,64,128]{2,1,0:T(8,128)S(1)} collective-permute-done((f32[10,64,128]{2,1,0:T(8,128)S(1)}, f32[10,64,128]{2,1,0:T(8,128)S(1)}, u32[]{:S(2)}, u32[]{:S(2)}) %collective-permute-start.3) | collective-permute-done | bytes 327712 | tf_op jit(solution)/shard_map/ppermute | solution.py:13
  224.2 7.7 %collective-permute-done.5 = f32[10,64,128]{2,1,0:T(8,128)S(1)} collective-permute-done((f32[10,64,128]{2,1,0:T(8,128)S(1)}, f32[10,64,128]{2,1,0:T(8,128)S(1)}, u32[]{:S(2)}, u32[]{:S(2)}) %collective-permute-start.5) | collective-permute-done | bytes 327712 | tf_op jit(solution)/shard_map/ppermute | solution.py:13
  232.3 1.1 convert_element_type.162
  233.5 6.5 %fusion.13 = (bf16[2,1,64,640]{2,1,3,0:T(2,128)(2,1)S(1)}, bf16[2,1,64,640]{2,1,3,0:T(2,128)(2,1)S(1)}, bf16[2,1,64,640]{2,1,3,0:T(2,128)(2,1)S(1)}, bf16[2,1,64,640]{2,1,3,0:T(2,128)(2,1)S(1)}) fusion(bf16[1,4,64,640]{2,1,3,0:T(4,128)(2,1)} %convert_element_type.162, bf16[1,4,64,640]{2,1,3,0:T(4,128)(2,1)} %copy.149), kind=kLoop, calls=%fused_computation.28 | loop fusion | flops 1310720 | bytes 1310720 | tf_op jit(solution)/shard_map/stack | solution.py:182
  240.0 1.0 copy.153
  242.2 0.9 pad_maximum_fusion.1
  243.2 4.0 %all-to-all-start.1 = ((bf16[4,2,1,64,640]{4,3,1,2,0:T(8,128)(2,1)}), bf16[4,2,1,64,640]{4,3,1,2,0:T(8,128)(2,1)S(1)}, u32[]{:S(2)}, u32[]{:S(2)}) async-start(bf16[4,2,1,64,640]{4,3,1,2,0:T(8,128)(2,1)} %pad_maximum_fusion.1), calls=%async_computation.1 | async-start | bytes 1310720 | tf_op jit(solution)/shard_map/all_to_all | solution.py:184
  247.8 1.0 add_bitcast_fusion
  248.8 8.6 %all-to-all-done.1 = bf16[4,2,1,64,640]{4,3,1,2,0:T(8,128)(2,1)S(1)} async-done(((bf16[4,2,1,64,640]{4,3,1,2,0:T(8,128)(2,1)}), bf16[4,2,1,64,640]{4,3,1,2,0:T(8,128)(2,1)S(1)}, u32[]{:S(2)}, u32[]{:S(2)}) %all-to-all-start.1) | async-done | bytes 655392 | tf_op jit(solution)/shard_map/all_to_all | solution.py:184
  259.1 0.8 multiply_convert_fusion.5
  (90 shorter events, 10.6 us)
Async XLA Ops:
  7.2 157.3 %all-gather.3.cloned.1.call-start = ((), (), s32[]{:S(2)}) async-start(), calls=%async_computation.2 | async-start | bytes 10303488 | tf_op jit(solution)/shard_map/all_gather | solution.py:52
  11.6 4.3 %copy-start.6 = (s32[64]{0:T(128)S(1)}, s32[64]{0:T(128)}, u32[]{:S(2)}) copy-start(s32[64]{0:T(128)} %param.23) | copy-start | bytes 772
  11.6 11.8 %copy-start.2 = (f32[4,2816]{1,0:T(4,128)S(1)}, f32[4,2816]{1,0:T(4,128)}, u32[]{:S(2)}) copy-start(f32[4,2816]{1,0:T(4,128)} %param.17) | copy-start | bytes 135172
  11.6 11.8 %slice-start = ((f32[4,2816]{1,0:T(4,128)}), f32[4,256]{1,0:T(4,128)S(1)}, s32[]{:S(2)}) async-start(f32[4,2816]{1,0:T(4,128)} %param.17), calls=%async_computation.3 | async-start | bytes 8192 | tf_op jit(solution)/shard_map/slice | solution.py:61
  11.6 166.6 %all-to-all-start = ((bf16[4,64,2560]{2,1,0:T(8,128)(2,1)}), bf16[4,64,2560]{2,1,0:T(8,128)(2,1)S(1)}, u32[]{:S(2)}, u32[]{:S(2)}) async-start(bf16[4,64,2560]{2,1,0:T(8,128)(2,1)} %broadcast_in_dim.39), calls=%async_computation | async-start | bytes 2621440 | tf_op jit(solution)/shard_map/all_to_all | solution.py:45
  178.2 5.9 %copy-start.4 = (f32[10]{0:T(128)S(1)}, f32[10]{0:T(128)}, u32[]{:S(2)}) copy-start(f32[10]{0:T(128)} %param.19) | copy-start | bytes 124
  178.2 5.9 %copy-start.7 = (f32[10]{0:T(128)S(1)}, f32[10]{0:T(128)}, u32[]{:S(2)}) copy-start(f32[10]{0:T(128)} %param.20) | copy-start | bytes 124
  184.0 1.2 copy-start.5
  187.4 24.9 %collective-permute-start.4 = (f32[10]{0:T(128)S(1)}, f32[10]{0:T(128)S(1)}, u32[]{:S(2)}, u32[]{:S(2)}) collective-permute-start(f32[10]{0:T(128)S(1)} %exponential_multiply_fusion.1), channel_id=1, source_target_pairs={{0,8},{4,12},{8,16},{12,20},{16,24},{20,28},{24,32},{28,36},{32,40... | collective-permute-start | bytes 128 | tf_op jit(solution)/shard_map/ppermute | solution.py:13
  190.8 21.5 %collective-permute-start.2 = (f32[10]{0:T(128)S(1)}, f32[10]{0:T(128)S(1)}, u32[]{:S(2)}, u32[]{:S(2)}) collective-permute-start(f32[10]{0:T(128)S(1)} %exponential_multiply_fusion.1), channel_id=1, source_target_pairs={{0,4},{4,8},{8,12},{12,16},{16,20},{20,24},{24,28},{28,32},{32,36}... | collective-permute-start | bytes 128 | tf_op jit(solution)/shard_map/ppermute | solution.py:13
  193.8 4.9 %collective-permute-start = (bf16[3,896]{0,1:T(8,128)(2,1)S(1)}, bf16[3,896]{0,1:T(8,128)(2,1)S(1)}, u32[]{:S(2)}, u32[]{:S(2)}) collective-permute-start(bf16[3,896]{0,1:T(8,128)(2,1)S(1)} %slice.120), channel_id=1, source_target_pairs={{0,4},{4,8},{8,12},{12,16},{16,20},{20,24},{24,28},{28,32},{32,36}... | collective-permute-start | bytes 16136 | tf_op jit(solution)/shard_map/ppermute | solution.py:13
  201.3 11.1 %collective-permute-start.1 = (f32[10,64,128]{2,1,0:T(8,128)S(1)}, f32[10,64,128]{2,1,0:T(8,128)S(1)}, u32[]{:S(2)}, u32[]{:S(2)}) collective-permute-start(f32[10,64,128]{2,1,0:T(8,128)S(1)} %fusion.23), channel_id=1, source_target_pairs={{0,4},{4,8},{8,12},{12,16},{16,20},{20,24},{24,28},{28,32},{32,36}... | collective-permute-start | bytes 983048 | tf_op jit(solution)/shard_map/ppermute | solution.py:13
  205.7 18.5 %collective-permute-start.3 = (f32[10,64,128]{2,1,0:T(8,128)S(1)}, f32[10,64,128]{2,1,0:T(8,128)S(1)}, u32[]{:S(2)}, u32[]{:S(2)}) collective-permute-start(f32[10,64,128]{2,1,0:T(8,128)S(1)} %fusion.23), channel_id=1, source_target_pairs={{0,8},{4,12},{8,16},{12,20},{16,24},{20,28},{24,32},{28,36},{32,40... | collective-permute-start | bytes 983048 | tf_op jit(solution)/shard_map/ppermute | solution.py:13
  208.7 23.2 %collective-permute-start.5 = (f32[10,64,128]{2,1,0:T(8,128)S(1)}, f32[10,64,128]{2,1,0:T(8,128)S(1)}, u32[]{:S(2)}, u32[]{:S(2)}) collective-permute-start(f32[10,64,128]{2,1,0:T(8,128)S(1)} %fusion.23), channel_id=1, source_target_pairs={{0,12},{4,16},{8,20},{12,24},{16,28},{20,32},{24,36},{28,40},{32,4... | collective-permute-start | bytes 983048 | tf_op jit(solution)/shard_map/ppermute | solution.py:13
  211.4 20.7 %copy-start.8 = (f32[10]{0:T(128)S(1)}, f32[10]{0:T(128)}, u32[]{:S(2)}) copy-start(f32[10]{0:T(128)} %param.21) | copy-start | bytes 124
  241.0 1.2 copy-start.1
  241.8 5.9 %copy-start = (bf16[256,640]{0,1:T(8,128)(2,1)S(1)}, bf16[256,640]{0,1:T(8,128)(2,1)}, u32[]{:S(2)}) copy-start(bf16[256,640]{0,1:T(8,128)(2,1)} %get-tuple-element.24) | copy-start | bytes 983044
  243.2 14.1 %all-to-all-start.1 = ((bf16[4,2,1,64,640]{4,3,1,2,0:T(8,128)(2,1)}), bf16[4,2,1,64,640]{4,3,1,2,0:T(8,128)(2,1)S(1)}, u32[]{:S(2)}, u32[]{:S(2)}) async-start(bf16[4,2,1,64,640]{4,3,1,2,0:T(8,128)(2,1)} %pad_maximum_fusion.1), calls=%async_computation.1 | async-start | bytes 1310720 | tf_op jit(solution)/shard_map/all_to_all | solution.py:184
  258.4 0.7 copy-start.3
Sparse Core Ops, SparseCore 0:
  11.7 152.7 all-gather.2
